TPU v7x, 32 devices: a whole 2x2x4 slice. The times are simulated.
32 devices in a mesh: vocab: 8 (over z, y), grp: 4 (over x, core).
Axes of the slice: x: 2, y: 2, z: 4, core: 2. Of those that a mesh axis runs over, the one named last changes fastest.
Arguments:
- states: bfloat16 [4, 96, 4096], P('grp', 'vocab'), may hold values from -256 to 256
- target_ids: int32 [4, 96], P('grp', 'vocab'), may hold values from 0 to 65535
- lengths: int32 [4, 8], P('grp'), may hold values from 1 to 12, 72 in all within a row
- order: int32 [4, 8], replicated, may hold values from 0 to 7, each once within a row
- gain: float32 [4096], replicated, may hold values from 0.25 to 1.75
- head: bfloat16 [4096, 65536], P(None, 'vocab'), may hold values from -16 to 16
Outputs:
- log_prob: float32 [4, 96], P('grp', 'vocab')
- entropy: float32 [4, 96], P('grp', 'vocab')
- state_norm: float32 [4, 96], P('grp', 'vocab')
- peak_logit: float32 [4, 96], P('grp', 'vocab')
Inputs may be any that keep to these rules, and one draw needn't show every extreme that they name: `order`: each row is a permutation of 0 to 7. `lengths`: each row sums to 72.
All inputs are finite; a program needn't handle non-finite values.
Results may differ from a plain program's by a relative error of at most 0.011.
The roundings to bfloat16 on the way count: a program that leaves them out, or rounds other values in their place, can miss the bound.
Values may be sent and summed in bfloat16 or wider, within the bound.
No kernel may reach another device: no remote copies, remote signals or barrier semaphores. Data moves between devices by JAX's collectives and lax.ppermute only.
A program may use at most 256 MiB of HBM per device.

v0:
```python
import jax
import jax.numpy as jnp
from jax import lax
from jax.sharding import PartitionSpec as P

EPSILON = 1e-05


def normalize(block_states, gain):
    values = block_states.astype(jnp.float32)
    mean_square = jnp.mean(values * values, axis=-1)
    normed = (values * lax.rsqrt(mean_square + EPSILON)[:, None] * gain).astype(jnp.bfloat16)
    return (normed, jnp.sqrt(mean_square))


def score_rows(normed, columns, token_ids, offset):
    logits = jnp.dot(normed, columns, preferred_element_type=jnp.float32)
    local_max = jnp.max(logits, axis=1)
    width = columns.shape[1]
    within = token_ids - offset
    inside = (within >= 0) & (within < width)
    picked = jnp.take_along_axis(logits, jnp.clip(within, 0, width - 1)[:, None], axis=1)[:, 0]
    return (logits, local_max, jnp.where(inside, picked, 0.0))


def exp_sums(logits, center):
    weights = jnp.exp(logits - center[:, None])
    return (jnp.sum(weights, axis=1), jnp.sum(weights * logits, axis=1))


def route_blocks(terms, destination):
    blocks = terms.shape[1]
    one_hot = (destination[:, None] == jnp.arange(blocks, dtype=jnp.int32)[None, :]).astype(
        jnp.float32
    )
    return jnp.einsum("kj,ckr->cjr", one_hot, terms, precision=lax.Precision.HIGHEST)


def own_block(values, position, count):
    return lax.dynamic_slice_in_dim(values, position * count, count)


def shards(states, target_ids, lengths, order, gain, head):
    count = states.shape[1]
    vocab_size = lax.axis_size("vocab")
    group_size = lax.axis_size("grp")
    vocab_index = lax.axis_index("vocab")
    group_index = lax.axis_index("grp")
    own_order = lax.dynamic_index_in_dim(order, group_index, 0, keepdims=False)
    block_ids = jnp.arange(vocab_size, dtype=jnp.int32)
    source_block = jnp.sum(jnp.where(own_order == vocab_index, block_ids, 0))
    length_own = jnp.sum(jnp.where(block_ids == source_block, lengths[0], 0))
    gathered, gathered_ids = (
        lax.all_gather(states, ("vocab", "grp"), axis=1, tiled=True),
        lax.all_gather(target_ids, ("vocab", "grp"), axis=1, tiled=True),
    )
    normed, root_mean = normalize(gathered[0], gain)
    width = head.shape[1] // group_size
    columns = lax.dynamic_slice_in_dim(head, group_index * width, width, 1)
    offset = (vocab_index * group_size + group_index) * width
    logits, local_max, target_logit = score_rows(normed, columns, gathered_ids[0], offset)
    peak = lax.pmax(local_max, ("vocab", "grp"))
    totals, expected = exp_sums(logits, peak)
    blocks = vocab_size * group_size
    terms = jnp.stack([totals, expected, target_logit]).reshape(3, blocks, count)
    group_ids = jnp.arange(group_size, dtype=jnp.int32)[None, :]
    destination = (order.T * group_size + group_ids).reshape(blocks)
    moved = route_blocks(terms, destination).reshape(3, blocks * count)
    mine = lax.psum_scatter(moved, ("vocab", "grp"), scatter_dimension=1, tiled=True)
    position = source_block * group_size + group_index
    own_totals, own_expected, own_target = (mine[0], mine[1], mine[2])
    own_peak = own_block(peak, position, count)
    own_root = own_block(root_mean, position, count)
    keep = (jnp.arange(count, dtype=jnp.int32) < length_own).astype(jnp.float32)
    log_total = jnp.log(own_totals)
    log_prob = (own_target - own_peak - log_total) * keep
    entropy = (own_peak + log_total - own_expected / own_totals) * keep
    return (log_prob[None], entropy[None], (own_root * keep)[None], (own_peak * keep)[None])


def solution(mesh):
    in_specs = (
        P("grp", "vocab", None),
        P("grp", "vocab"),
        P("grp", None),
        P(),
        P(),
        P(None, "vocab"),
    )
    out_specs = (P("grp", "vocab"), P("grp", "vocab"), P("grp", "vocab"), P("grp", "vocab"))
    return jax.shard_map(shards, mesh=mesh, in_specs=in_specs, out_specs=out_specs, check_vma=False)
```

profile of v0, /device:TPU:0, one launch (start us, length us, event | category | flops | bytes accessed | tf_op | source)
XLA Modules:
  0.0 204.1 jit_solution(16833374858033421563)
XLA Ops:
  7.2 0.0 all-gather.2.cloned.1.call-start
  7.2 1.7 copy.16
  9.0 0.0 all-gather.2.cloned.1.call-update
  9.0 0.7 bitcast_add_fusion
  9.7 0.1 copy.20
  9.8 0.1 eq.35
  9.9 1.3 fusion.23
  11.9 0.8 bitcast_dynamic-update-slice_fusion
  12.6 42.2 %all-reduce = s32[384]{0:T(512)S(1)} all-reduce(s32[384]{0:T(512)S(1)} %bitcast_dynamic-update-slice_fusion), channel_id=1, replica_groups=mesh['vocab'=8,'grp'=4] {'vocab','grp'}, use_global_device_ids=true, to_apply=%add | all-reduce | flops 384 | bytes 3072
  54.8 2.0 fusion.22
  56.9 26.3 %all-gather.2.cloned.1.call-done = bf16[1,384,4096]{2,0,1:T(2,128)(2,1)} async-done(((bf16[1,12,4096]{2,0,1:T(2,128)(2,1)}), bf16[1,384,4096]{2,0,1:T(2,128)(2,1)}) %all-gather.2.cloned.1.call-update) | async-done | bytes 3145744 | tf_op jit(solution)/shard_map/all_gather | solution.py:54
  83.2 7.7 %convert_element_type.14 = f32[1,384,4096]{2,0,1:T(1,128)S(1)} convert(bf16[1,384,4096]{2,0,1:T(2,128)(2,1)} %all-gather.2.cloned.1.call-done) | non-fusion elementwise | flops 1572864 | bytes 9437184 | tf_op jit(solution)/shard_map/convert_element_type | solution.py:10
  90.9 0.0 copy-start
  90.9 3.3 %fusion.2 = f32[384]{0:T(512)S(1)} fusion(f32[1,384,4096]{2,0,1:T(1,128)S(1)} %convert_element_type.14), kind=kLoop, calls=%fused_computation.5 | loop fusion | flops 3145344 | bytes 6292992 | tf_op jit(solution)/shard_map/reduce_sum | solution.py:11
  94.3 0.0 copy-done
  94.3 15.6 %fusion.30 = (f32[384]{0:T(512)S(1)}, f32[384,2048]{1,0:T(8,128)S(1)}) fusion(bf16[4096,8192]{1,0:T(8,128)(2,1)} %param.11, s32[]{:T(128)S(6)} %select_n.61, f32[1,384,4096]{2,0,1:T(1,128)S(1)} %convert_element_type.14, f32[4096]{0:T(1024)S(1)} %copy-done, f32[384]{0:T(512)S(1)} %get-tuple-element.10), kind=kOutput, calls=%fused_computation.59 | convolution fusion | flops 6447955456 | bytes 26233860 | tf_op jit(solution)/shard_map/dot_general | solution.py:17
  109.8 3.5 %gather_fusion = f32[384]{0:T(512)S(1)} fusion(f32[384,2048]{1,0:T(8,128)S(1)} %get-tuple-element.12, s32[384]{0:T(512)S(1)} %fusion.21), kind=kCustom, calls=%fused_computation | custom fusion | bytes 6144 | tf_op jit(solution)/shard_map/jit(take_along_axis)/gather | solution.py:22
  113.3 0.1 stack.14
  113.4 0.1 copy.19
  113.5 39.4 %pmax.7 = f32[384]{0:T(512)S(1)} all-reduce(f32[384]{0:T(512)S(1)} %get-tuple-element.11), channel_id=1, replica_groups=mesh['vocab'=8,'grp'=4] {'vocab','grp'}, use_global_device_ids=true, to_apply=%region_4.5 | all-reduce | flops 384 | bytes 3072 | tf_op jit(solution)/shard_map/pmax | solution.py:62
  152.9 1.0 fusion.6
  153.9 0.1 stack.12
  154.0 0.1 copy.17
  154.1 0.1 stack.13
  154.2 0.1 copy.18
  154.3 0.2 convolution_bitcast_fusion
  154.5 0.1 copy.21
  154.6 0.1 reshape.85
  154.7 40.0 %all-reduce.1 = f32[3,384]{1,0:T(4,128)S(1)} all-reduce(f32[3,384]{1,0:T(4,128)S(1)} %reshape.85), channel_id=2, replica_groups=mesh['vocab'=8,'grp'=4] {'vocab','grp'}, use_global_device_ids=true, to_apply=%region_7.8.clone | all-reduce | flops 1152 | bytes 9216
  194.7 0.1 constant_dynamic-slice_fusion
  194.8 1.2 fusion.25
  196.0 1.2 select_bitcast_fusion.1
  (9 shorter events, 0.1 us)
Async XLA Ops:
  7.2 76.0 %all-gather.2.cloned.1.call-start = ((), (), s32[]{:S(2)}) async-start(), calls=%async_computation | async-start | bytes 6488064 | tf_op jit(solution)/shard_map/all_gather | solution.py:54
  90.9 3.3 %copy-start = (f32[4096]{0:T(1024)S(1)}, f32[4096]{0:T(1024)}, u32[]{:S(2)}) copy-start(f32[4096]{0:T(1024)} %param.10) | copy-start | bytes 49156
Sparse Core Ops, SparseCore 0:
  10.9 72.2 all-gather.1
where the time goes:
time: 205 us; the launch traced here: 204 us
  blocking collectives  122 us (60%)
  waiting for transfers between devices  26.3 us (13%)
  other arithmetic  18.6 us (9%)
  matrix products  15.8 us (8%)
  between operations  14.8 us (7%)
  local copies, waits for them, and re-layouts  6.96 us (3%)
    unnamed x2, blocking collectives  82.2 us
    pmax x1, blocking collectives, shards(): peak = lax.pmax(local_max, ('vocab', 'grp'))  39.4 us
    all_gather x1, waiting for transfers between devices, shards(): lax.all_gather(states, ('vocab', 'grp'), axis=1, tiled=True)  26.3 us
    dot_general x1, matrix products, score_rows(): logits = jnp.dot(normed, columns, preferred_element_type=jnp.float32)  15.6 us
    convert_element_type x1, other arithmetic, normalize(): values = block_states.astype(jnp.float32)  7.72 us
  transfers between devices with their start and end apart: 1, of which 1 were waited for; matrix products, arithmetic and copies ran while one was open for 2% of the time, Pallas kernels for 0%

commit v1 on v0

--- a/solution.py
+++ b/solution.py
@@ -4,6 +4,18 @@
 from jax.sharding import PartitionSpec as P
 
 EPSILON = 1e-05
+
+
+def doubled_up(value, axis, dim):
+    ways, here = (lax.axis_size(axis), lax.axis_index(axis))
+    grown, reach = (value, 1)
+    while reach < ways:
+        theirs = lax.ppermute(grown, axis, [(d, d ^ reach) for d in range(ways)])
+        mine_first = jnp.concatenate([grown, theirs], axis=dim)
+        theirs_first = jnp.concatenate([theirs, grown], axis=dim)
+        grown = jnp.where(here & reach == 0, mine_first, theirs_first)
+        reach = 2 * reach
+    return grown
 
 
 def normalize(block_states, gain):
@@ -51,7 +63,7 @@
     source_block = jnp.sum(jnp.where(own_order == vocab_index, block_ids, 0))
     length_own = jnp.sum(jnp.where(block_ids == source_block, lengths[0], 0))
     gathered, gathered_ids = (
-        lax.all_gather(states, ("vocab", "grp"), axis=1, tiled=True),
+        doubled_up(states, ("vocab", "grp"), 1),
         lax.all_gather(target_ids, ("vocab", "grp"), axis=1, tiled=True),
     )
     normed, root_mean = normalize(gathered[0], gain)

time: 205 us -> 238 us (1.16)
  blocking collectives: 122 us -> 168 us
  between operations: 14.8 us -> 1.48 us
  starting transfers between devices: 0.04 us -> 9.02 us
  other arithmetic: 18.6 us -> 11 us
  waiting for transfers between devices: 26.3 us -> 28.7 us
    unnamed x2, blocking collectives: 82.2 us -> 130 us
    ppermute x0 -> x5, waiting for transfers between devices: none -> 28.7 us  [doubled_up(): theirs = lax.ppermute(grown, axis, [(d, d ^ reach) for d in range(ways)])]
    all_gather x1 -> x0, waiting for transfers between devices: 26.3 us -> none  [shards(): lax.all_gather(states, ('vocab', 'grp'), axis=1, tiled=True)]
    ppermute x0 -> x5, starting transfers between devices: none -> 9.02 us  [doubled_up(): theirs = lax.ppermute(grown, axis, [(d, d ^ reach) for d in range(ways)])]
    convert_element_type x1 -> x0, other arithmetic: 7.72 us -> none  [normalize(): values = block_states.astype(jnp.float32)]
    select_n x0 -> x8, other arithmetic: none -> 4.39 us  [doubled_up(): grown = jnp.where(here & reach == 0, mine_first, theirs_first)]
    unnamed x7 -> x16, local copies, waits for them, and re-layouts: 2.59 us -> 0.19 us
  transfers between devices with their start and end apart: 1 -> 5, of which waited for: 1 -> 4; matrix products, arithmetic and copies ran while one was open for 2% -> 2% of each run, Pallas kernels for 0% -> 0%
where the time goes in v1:
time: 238 us
  blocking collectives  168 us (71%)
  waiting for transfers between devices  28.7 us (12%)
  matrix products  13.9 us (6%)
  other arithmetic  11 us (5%)
  starting transfers between devices  9.02 us (4%)
  local copies, waits for them, and re-layouts  5.08 us (2%)
    unnamed x2, blocking collectives  130 us
    pmax x1, blocking collectives, shards(): peak = lax.pmax(local_max, ('vocab', 'grp'))  38.5 us
    ppermute x5, waiting for transfers between devices, doubled_up(): theirs = lax.ppermute(grown, axis, [(d, d ^ reach) for d in range(ways)])  28.7 us
    dot_general x1, matrix products, score_rows(): logits = jnp.dot(normed, columns, preferred_element_type=jnp.float32)  13.7 us
    ppermute x5, starting transfers between devices, doubled_up(): theirs = lax.ppermute(grown, axis, [(d, d ^ reach) for d in range(ways)])  9.02 us
  transfers between devices with their start and end apart: 5, of which 4 were waited for; matrix products, arithmetic and copies ran while one was open for 2% of the time, Pallas kernels for 0%

profile of v1, /device:TPU:0, one launch (start us, length us, event | category | flops | bytes accessed | tf_op | source)
XLA Modules:
  0.0 237.6 jit_solution(16231625244575135528)
XLA Ops:
  0.6 0.0 copy-start.1
  0.6 0.5 collective-permute-start
  1.2 1.2 collective-permute-done
  2.4 1.1 maximum_select_fusion.9
  3.4 2.9 %collective-permute-start.1 = (bf16[1,24,4096]{2,1,0:T(8,128)(2,1)S(1)}, bf16[1,24,4096]{2,1,0:T(8,128)(2,1)S(1)}, u32[]{:S(2)}, u32[]{:S(2)}) collective-permute-start(bf16[1,24,4096]{2,1,0:T(8,128)(2,1)S(1)} %maximum_select_fusion.9), channel_id=1, source_target_pairs={{0,2},{1,3},{2,0},{3,1},{4,6},{5,7},{6,4},{7,5},{8,10},{9,11},{10,... | collective-permute-start | bytes 589832 | tf_op jit(solution)/shard_map/ppermute | solution.py:13
  6.4 1.1 maximum_select_fusion.8
  7.5 4.1 %collective-permute-done.1 = bf16[1,24,4096]{2,1,0:T(8,128)(2,1)S(1)} collective-permute-done((bf16[1,24,4096]{2,1,0:T(8,128)(2,1)S(1)}, bf16[1,24,4096]{2,1,0:T(8,128)(2,1)S(1)}, u32[]{:S(2)}, u32[]{:S(2)}) %collective-permute-start.1) | collective-permute-done | bytes 196640 | tf_op jit(solution)/shard_map/ppermute | solution.py:13
  11.6 0.1 maximum_select_fusion.7
  11.6 1.8 collective-permute-start.2
  13.5 0.1 maximum_select_fusion.6
  13.6 8.8 %collective-permute-done.2 = bf16[1,48,4096]{2,1,0:T(8,128)(2,1)S(1)} collective-permute-done((bf16[1,48,4096]{2,1,0:T(8,128)(2,1)S(1)}, bf16[1,48,4096]{2,1,0:T(8,128)(2,1)S(1)}, u32[]{:S(2)}, u32[]{:S(2)}) %collective-permute-start.2) | collective-permute-done | bytes 393248 | tf_op jit(solution)/shard_map/ppermute | solution.py:13
  22.4 0.0 copy-start.4
  22.4 0.0 copy-start.5
  22.4 0.1 maximum_select_fusion.4
  22.5 1.6 collective-permute-start.3
  24.1 0.0 copy-done.1
  24.1 0.1 copy.19
  24.2 0.6 eq.55
  24.8 0.6 fusion.23
  26.1 0.1 maximum_select_fusion.3
  26.3 14.5 %collective-permute-done.3 = bf16[1,96,4096]{2,1,0:T(8,128)(2,1)S(1)} collective-permute-done((bf16[1,96,4096]{2,1,0:T(8,128)(2,1)S(1)}, bf16[1,96,4096]{2,1,0:T(8,128)(2,1)S(1)}, u32[]{:S(2)}, u32[]{:S(2)}) %collective-permute-start.3) | collective-permute-done | bytes 786464 | tf_op jit(solution)/shard_map/ppermute | solution.py:13
  40.8 1.5 maximum_select_fusion.2
  42.3 2.2 collective-permute-start.4
  44.4 0.0 copy-done.4
  44.4 0.1 bitcast_dynamic-update-slice_fusion
  44.5 88.3 %all-reduce = s32[384]{0:T(512)S(1)} all-reduce(s32[384]{0:T(512)S(1)} %bitcast_dynamic-update-slice_fusion), channel_id=1, replica_groups=mesh['vocab'=8,'grp'=4] {'vocab','grp'}, use_global_device_ids=true, to_apply=%add | all-reduce | flops 384 | bytes 3072
  132.8 0.0 copy-done.5
  132.8 1.3 fusion.22
  134.2 0.0 copy-start.3
  134.2 0.3 maximum_select_fusion.1
  134.5 0.0 collective-permute-done.4
  134.5 0.0 copy-start
  134.5 1.2 fusion.2
  135.8 0.0 copy-done
  135.8 0.0 copy-done.3
  135.8 13.7 %fusion.31 = (f32[384]{0:T(512)S(1)}, f32[384,2048]{1,0:T(8,128)S(1)}) fusion(bf16[4096,8192]{1,0:T(8,128)(2,1)} %param.11, s32[]{:T(128)S(6)} %select_n.205, f32[4096]{0:T(1024)S(1)} %copy-done.3, f32[384]{0:T(512)S(1)} %get-tuple-element.10, bf16[192,4096]{1,0:T(8,128)(2,1)S(1)} %maximum_select_fusion.1, bf16[192,4096]{1,0:T(8,128)(2,1)} %bitcast.60, ...), kind=kOutput, calls=%fused_computation.69 | convolution fusion | flops 6463684096 | bytes 23088132 | tf_op jit(solution)/shard_map/dot_general | solution.py:29
  149.6 0.0 copy-start.2
  149.6 38.5 %pmax.7 = f32[384]{0:T(512)S(1)} all-reduce(f32[384]{0:T(512)S(1)} %get-tuple-element.11), channel_id=1, replica_groups=mesh['vocab'=8,'grp'=4] {'vocab','grp'}, use_global_device_ids=true, to_apply=%region_4.5 | all-reduce | flops 384 | bytes 3072 | tf_op jit(solution)/shard_map/pmax | solution.py:74
  188.0 1.0 fusion.6
  189.0 0.1 stack.12
  189.1 0.1 copy.16
  189.2 0.1 stack.13
  189.3 0.1 copy.17
  189.4 3.5 %gather_fusion = f32[384]{0:T(512)S(1)} fusion(f32[384,2048]{1,0:T(8,128)S(1)} %get-tuple-element.12, s32[384]{0:T(512)S(1)} %fusion.21), kind=kCustom, calls=%fused_computation | custom fusion | bytes 6144 | tf_op jit(solution)/shard_map/jit(take_along_axis)/gather | solution.py:34
  192.9 0.1 stack.14
  193.0 0.1 copy.18
  193.1 0.0 copy-done.2
  193.1 0.2 convolution_bitcast_fusion
  193.3 0.1 copy.20
  193.4 0.1 reshape.520
  193.5 41.7 %all-reduce.1 = f32[3,384]{1,0:T(4,128)S(1)} all-reduce(f32[3,384]{1,0:T(4,128)S(1)} %reshape.520), channel_id=2, replica_groups=mesh['vocab'=8,'grp'=4] {'vocab','grp'}, use_global_device_ids=true, to_apply=%region_7.8.clone | all-reduce | flops 1152 | bytes 9216
  235.1 0.1 constant_dynamic-slice_fusion
  235.2 1.2 fusion.25
  236.4 1.2 select_bitcast_fusion.1
  (10 shorter events, 0.1 us)
Async XLA Ops:
  0.6 23.5 %copy-start.1 = (s32[4,8]{1,0:T(4,128)S(1)}, s32[4,8]{1,0:T(4,128)}, u32[]{:S(2)}) copy-start(s32[4,8]{1,0:T(4,128)} %param.9) | copy-start | bytes 388
  0.6 1.7 collective-permute-start
  3.4 8.1 %collective-permute-start.1 = (bf16[1,24,4096]{2,1,0:T(8,128)(2,1)S(1)}, bf16[1,24,4096]{2,1,0:T(8,128)(2,1)S(1)}, u32[]{:S(2)}, u32[]{:S(2)}) collective-permute-start(bf16[1,24,4096]{2,1,0:T(8,128)(2,1)S(1)} %maximum_select_fusion.9), channel_id=1, source_target_pairs={{0,2},{1,3},{2,0},{3,1},{4,6},{5,7},{6,4},{7,5},{8,10},{9,11},{10,... | collective-permute-start | bytes 589832 | tf_op jit(solution)/shard_map/ppermute | solution.py:13
  11.6 10.7 %collective-permute-start.2 = (bf16[1,48,4096]{2,1,0:T(8,128)(2,1)S(1)}, bf16[1,48,4096]{2,1,0:T(8,128)(2,1)S(1)}, u32[]{:S(2)}, u32[]{:S(2)}) collective-permute-start(bf16[1,48,4096]{2,1,0:T(8,128)(2,1)S(1)} %maximum_select_fusion.7), channel_id=1, source_target_pairs={{0,4},{1,5},{2,6},{3,7},{4,0},{5,1},{6,2},{7,3},{8,12},{9,13},{10,... | collective-permute-start | bytes 1179656 | tf_op jit(solution)/shard_map/ppermute | solution.py:13
  22.4 22.1 %copy-start.4 = (s32[1,12]{1,0:T(1,128)S(1)}, s32[1,12]{1,0:T(1,128)}, u32[]{:S(2)}) copy-start(s32[1,12]{1,0:T(1,128)} %param.7) | copy-start | bytes 148
  22.4 110.5 %copy-start.5 = (s32[1,8]{1,0:T(1,128)S(1)}, s32[1,8]{1,0:T(1,128)}, u32[]{:S(2)}) copy-start(s32[1,8]{1,0:T(1,128)} %param.8) | copy-start | bytes 100
  22.5 18.2 %collective-permute-start.3 = (bf16[1,96,4096]{2,1,0:T(8,128)(2,1)S(1)}, bf16[1,96,4096]{2,1,0:T(8,128)(2,1)S(1)}, u32[]{:S(2)}, u32[]{:S(2)}) collective-permute-start(bf16[1,96,4096]{2,1,0:T(8,128)(2,1)S(1)} %maximum_select_fusion.4), channel_id=1, source_target_pairs={{0,8},{1,9},{2,10},{3,11},{4,12},{5,13},{6,14},{7,15},{8,0},{9,1},... | collective-permute-start | bytes 2359304 | tf_op jit(solution)/shard_map/ppermute | solution.py:13
  42.3 92.3 %collective-permute-start.4 = (bf16[1,192,4096]{2,1,0:T(8,128)(2,1)}, bf16[1,192,4096]{2,1,0:T(8,128)(2,1)S(1)}, u32[]{:S(2)}, u32[]{:S(2)}) collective-permute-start(bf16[1,192,4096]{2,1,0:T(8,128)(2,1)} %maximum_select_fusion.2), channel_id=1, source_target_pairs={{0,16},{1,17},{2,18},{3,19},{4,20},{5,21},{6,22},{7,23},{8,24},{9,... | collective-permute-start | bytes 4718600 | tf_op jit(solution)/shard_map/ppermute | solution.py:13
  134.2 1.6 copy-start.3
  134.5 1.3 copy-start
  149.6 43.5 %copy-start.2 = (s32[32]{0:T(128)S(1)}, s32[32]{0:T(128)}, u32[]{:S(2)}) copy-start(s32[32]{0:T(128)} %eq.55) | copy-start | bytes 388
